TPU v7x, 512 devices: a whole 4x8x8 slice. The times are simulated.
512 devices in a mesh: seq: 128 (over y, z, core), tp: 4 (over x).
Axes of the slice: x: 4, y: 8, z: 8, core: 2. Of those that a mesh axis runs over, the one named last changes fastest.
Arguments:
- tokens: bfloat16 [32768, 1280], P('seq', 'tp'), may hold values from -6 to 6
- first_gain: float32 [1280], replicated, may hold values from 0.1 to 1.9
- w_query: bfloat16 [1280, 1280], P(None, 'tp')
- w_key: bfloat16 [1280, 1280], P(None, 'tp')
- w_value: bfloat16 [1280, 1280], P(None, 'tp'), may hold values from -0.15625 to 0.15625
- w_out: bfloat16 [1280, 1280], P('tp'), may hold values from -0.625 to 0.625
- segment_ids: int32 [32768], P('seq'), may hold values from 0 to 191, never falling along the last dimension, each value on 1 to 512 neighbouring positions
- keep_mask: int32 [32768], P('seq'), may hold values 0 or 1
- merge_gain: float32 [1280], replicated, may hold values from 0.1 to 1.9
- w_merge: bfloat16 [5120, 640], P('tp'), may hold values from -0.078125 to 0.078125
- merge_index: int32 [8192, 4], P('seq'), may hold values from 0 to 32767, as said below
- destination: int32 [8192], P('seq'), may hold values from 0 to 8191, as said below
Outputs:
- delivered: bfloat16 [8192, 640], P('seq', 'tp')
Inputs may be any that keep to these rules, and one draw needn't show every extreme that they name: `segment_ids`: segment numbers never fall along the tokens; each picture or clip holds 1 to 512 tokens and one holds exactly 512. `merge_index`: the four entries of merged row m are different tokens of the device that holds row m, that is of rows (m // 64) * 256 to that plus 256 - 1; every token lies in exactly one group. `destination`: a permutation of the merged rows. The owner of row m is destination[m] // 64; the 64 rows of each device go to exactly 32 owners, exactly 2 rows to each.
All inputs are finite; a program needn't handle non-finite values. No bound on the sum of `keep_mask` on one device may be relied on, other than what follows from the above.
Results may differ from a plain program's by a relative error of at most 0.022.
Values may be sent and summed in bfloat16 or wider, within the bound.
No kernel may reach another device: no remote copies, remote signals or barrier semaphores. Data moves between devices by JAX's collectives and lax.ppermute only.
A program may use at most 64 MiB of HBM per device.

v0:
```python
import jax
import jax.numpy as jnp
from jax import lax
from jax.sharding import PartitionSpec as P

HD = 80
CAP = 2
EPS = 1e-06


def from_behind(shard, axis, by):
    length = lax.axis_size(axis)
    pairs = [(i, i + by) for i in range(length) if 0 <= i + by < length]
    return lax.ppermute(shard, axis, pairs)


def layer_norm(activations, norm_gain):
    activations = activations.astype(jnp.float32)
    row_mean = jnp.mean(activations, axis=-1, keepdims=True)
    centered = activations - row_mean
    variance = jnp.mean(centered * centered, axis=-1, keepdims=True)
    return centered * lax.rsqrt(variance + EPS) * norm_gain


def body(
    tokens,
    first_gain,
    w_query,
    w_key,
    w_value,
    w_out,
    segment_ids,
    keep_mask,
    merge_gain,
    w_merge,
    merge_index,
    destination,
):
    row_count = tokens.shape[0]
    local_width = w_query.shape[1]
    heads_here = local_width // HD
    tp_size = lax.axis_size("tp")
    seq_size = lax.axis_size("seq")
    gathered = lax.all_gather(tokens, "tp", axis=1, tiled=True)
    normed = layer_norm(gathered, first_gain).astype(jnp.bfloat16)
    queries = jnp.dot(normed, w_query, preferred_element_type=jnp.float32).astype(jnp.bfloat16)
    key_rows = jnp.dot(normed, w_key, preferred_element_type=jnp.float32).astype(jnp.bfloat16)
    value_rows = jnp.dot(normed, w_value, preferred_element_type=jnp.float32).astype(jnp.bfloat16)
    paired = jnp.concatenate([key_rows, value_rows], axis=1)
    code_query = segment_ids + 1
    code_key = jnp.where(keep_mask > 0, code_query, 0)
    pair_list = [paired]
    code_list = [code_key]
    for offset in (1, 2, -1, -2):
        moved_pair, moved_code = from_behind((paired, code_key), "seq", offset)
        pair_list.append(moved_pair)
        code_list.append(moved_code)
    all_pairs = jnp.concatenate(pair_list, axis=0)
    all_codes = jnp.concatenate(code_list, axis=0)
    window = all_pairs.shape[0]
    key_heads = all_pairs[:, :local_width].reshape(window, heads_here, HD)
    value_heads = all_pairs[:, local_width:].reshape(window, heads_here, HD)
    query_heads = queries.reshape(row_count, heads_here, HD)
    score_scale = HD ** (-0.5)
    scores = (
        jnp.einsum("qhd,khd->hqk", query_heads, key_heads, preferred_element_type=jnp.float32)
        * score_scale
    )
    query_pos = jnp.arange(row_count)[:, None]
    key_pos = jnp.arange(window)[None, :]
    allowed = (code_query[:, None] == all_codes[None, :]) | (key_pos == query_pos)
    scores = jnp.where(allowed[None], scores, -1e30)
    row_max = jnp.max(scores, axis=-1, keepdims=True)
    exponent = jnp.exp(scores - row_max)
    row_total = jnp.sum(exponent, axis=-1, keepdims=True)
    weights = (exponent / row_total).astype(jnp.bfloat16)
    attended = jnp.einsum("hqk,khd->qhd", weights, value_heads, preferred_element_type=jnp.float32)
    attended = attended.reshape(row_count, local_width).astype(jnp.bfloat16)
    position = lax.axis_index("tp")
    seq_index = lax.axis_index("seq")
    local_index = merge_index - seq_index * row_count
    order = local_index.T.reshape(row_count)
    attended_sorted = jnp.take(attended, order, axis=0)
    partial_sum = jnp.dot(attended_sorted, w_out, preferred_element_type=jnp.float32)
    mixed_sum = lax.psum_scatter(
        partial_sum.astype(jnp.bfloat16), "tp", scatter_dimension=0, tiled=True
    ).astype(jnp.float32)
    column = lax.dynamic_slice_in_dim(local_index, position, 1, 1)[:, 0]
    residual = jnp.take(gathered, column, axis=0)
    updated = residual.astype(jnp.float32) + mixed_sum
    picked = layer_norm(updated, merge_gain).astype(jnp.bfloat16)
    partial_proj = jnp.dot(picked, w_merge, preferred_element_type=jnp.float32)
    projected = lax.psum_scatter(
        partial_proj.astype(jnp.bfloat16), "tp", scatter_dimension=1, tiled=True
    )
    slot_count = projected.shape[0]
    width = projected.shape[1]
    owner = destination // slot_count
    slot = destination - owner * slot_count
    lane = jnp.arange(slot_count)
    same_owner = owner[:, None] == owner[None, :]
    earlier = lane[None, :] < lane[:, None]
    rank = jnp.sum(jnp.where(same_owner & earlier, 1, 0), axis=1)
    send_pos = owner * CAP + rank
    target = jnp.arange(seq_size * CAP)
    send_hot = (send_pos[None, :] == target[:, None]).astype(jnp.bfloat16)
    send_rows = jnp.dot(send_hot, projected, preferred_element_type=jnp.float32)
    send_rows = send_rows.astype(jnp.bfloat16).reshape(seq_size, CAP, width)
    slot_code = (slot + 1).astype(jnp.float32)
    send_slot = jnp.dot(send_hot.astype(jnp.float32), slot_code, precision=lax.Precision.HIGHEST)
    slot_row = jnp.zeros((seq_size, 1, width), jnp.bfloat16)
    slot_row = slot_row.at[:, 0, :CAP].set(send_slot.reshape(seq_size, CAP).astype(jnp.bfloat16))
    send_buf = jnp.concatenate([send_rows, slot_row], axis=1).reshape(seq_size * (CAP + 1), width)
    recv = lax.all_to_all(send_buf, "seq", 0, 0, tiled=True).reshape(seq_size, CAP + 1, width)
    recv_rows = recv[:, :CAP, :].reshape(seq_size * CAP, width)
    recv_slot = recv[:, CAP, :CAP].reshape(seq_size * CAP).astype(jnp.int32) - 1
    recv_hot = (recv_slot[None, :] == lane[:, None]).astype(jnp.bfloat16)
    delivered = jnp.dot(recv_hot, recv_rows, preferred_element_type=jnp.float32)
    return delivered.astype(jnp.bfloat16)


def solution(mesh):
    return jax.shard_map(
        body,
        mesh=mesh,
        in_specs=(
            P("seq", "tp"),
            P(),
            P(None, "tp"),
            P(None, "tp"),
            P(None, "tp"),
            P("tp", None),
            P("seq"),
            P("seq"),
            P(),
            P("tp", None),
            P("seq", None),
            P("seq"),
        ),
        out_specs=P("seq", "tp"),
        check_vma=False,
    )
```

profile of v0, /device:TPU:1, one launch (start us, length us, event | category | flops | bytes accessed | tf_op | source)
XLA Modules:
  0.0 177.3 jit_solution(7128493967322918882)
XLA Ops:
  6.5 11.7 %all_gather.3 = bf16[256,1280]{0,1:T(8,128)(2,1)S(1)} all-gather(bf16[256,320]{0,1:T(8,128)(2,1)} %param.14), channel_id=1, replica_groups=mesh['seq'=128,'tp'=4] {'tp'}, dimensions={1}, use_global_device_ids=true | all-gather | bytes 819200 | tf_op jit(solution)/shard_map/all_gather | solution.py:44
  20.1 0.9 pad_maximum_fusion
  20.9 7.4 %collective-permute-start = (bf16[256,640]{0,1:T(8,128)(2,1)}, bf16[256,640]{0,1:T(8,128)(2,1)}, u32[]{:S(2)}, u32[]{:S(2)}) collective-permute-start(bf16[256,640]{0,1:T(8,128)(2,1)} %get-tuple-element.23), channel_id=1, source_target_pairs={{0,4},{4,8},{8,12},{12,16},{16,20},{20,24},{24,28},{28,32},{32,36}... | collective-permute-start | bytes 983048 | tf_op jit(solution)/shard_map/ppermute | solution.py:14
  28.4 4.0 %collective-permute-start.1 = (bf16[256,640]{0,1:T(8,128)(2,1)}, bf16[256,640]{0,1:T(8,128)(2,1)S(1)}, u32[]{:S(2)}, u32[]{:S(2)}) collective-permute-start(bf16[256,640]{0,1:T(8,128)(2,1)} %get-tuple-element.23), channel_id=1, source_target_pairs={{0,8},{4,12},{8,16},{12,20},{16,24},{20,28},{24,32},{28,36},{32,40... | collective-permute-start | bytes 983048 | tf_op jit(solution)/shard_map/ppermute | solution.py:14
  32.4 2.3 %collective-permute-start.2 = (bf16[256,640]{0,1:T(8,128)(2,1)}, bf16[256,640]{0,1:T(8,128)(2,1)S(1)}, u32[]{:S(2)}, u32[]{:S(2)}) collective-permute-start(bf16[256,640]{0,1:T(8,128)(2,1)} %get-tuple-element.23), channel_id=1, source_target_pairs={{4,0},{8,4},{12,8},{16,12},{20,16},{24,20},{28,24},{32,28},{36,32}... | collective-permute-start | bytes 983048 | tf_op jit(solution)/shard_map/ppermute | solution.py:14
  34.7 1.3 collective-permute-start.3
  36.1 3.9 %collective-permute-start.4 = (s32[256]{0:T(256)S(1)}, s32[256]{0:T(256)S(1)}, u32[]{:S(2)}, u32[]{:S(2)}) collective-permute-start(s32[256]{0:T(256)S(1)} %get-tuple-element.20), channel_id=1, source_target_pairs={{0,4},{4,8},{8,12},{12,16},{16,20},{20,24},{24,28},{28,32},{32,36}... | collective-permute-start | bytes 3080 | tf_op jit(solution)/shard_map/ppermute | solution.py:14
  40.2 2.4 %convolution_convert_fusion.1 = bf16[256,320]{0,1:T(8,128)(2,1)} fusion(bf16[1280,320]{0,1:T(8,128)(2,1)} %param.16, bf16[256,1280]{0,1:T(8,128)(2,1)S(1)} %all_gather.3, f32[1280]{0:T(1024)S(1)} %copy-done.10, f32[256]{0:T(256)S(1)} %add_rsqrt_fusion, f32[256]{0:T(256)S(1)} %broadcast_multiply_fusion), kind=kOutput, calls=%fused_computation.23 | convolution fusion | flops 211435520 | bytes 1645568 | tf_op jit(solution)/shard_map/dot_general | solution.py:46
  42.6 4.0 %collective-permute-start.5 = (s32[256]{0:T(256)S(1)}, s32[256]{0:T(256)S(1)}, u32[]{:S(2)}, u32[]{:S(2)}) collective-permute-start(s32[256]{0:T(256)S(1)} %get-tuple-element.20), channel_id=1, source_target_pairs={{0,8},{4,12},{8,16},{12,20},{16,24},{20,28},{24,32},{28,36},{32,40... | collective-permute-start | bytes 3080 | tf_op jit(solution)/shard_map/ppermute | solution.py:14
  46.6 0.7 collective-permute-done.5
  47.3 1.9 %collective-permute-start.6 = (s32[256]{0:T(256)S(1)}, s32[256]{0:T(256)S(1)}, u32[]{:S(2)}, u32[]{:S(2)}) collective-permute-start(s32[256]{0:T(256)S(1)} %get-tuple-element.20), channel_id=1, source_target_pairs={{4,0},{8,4},{12,8},{16,12},{20,16},{24,20},{28,24},{32,28},{36,32}... | collective-permute-start | bytes 3080 | tf_op jit(solution)/shard_map/ppermute | solution.py:14
  49.2 4.0 %collective-permute-done.6 = s32[256]{0:T(256)S(1)} collective-permute-done((s32[256]{0:T(256)S(1)}, s32[256]{0:T(256)S(1)}, u32[]{:S(2)}, u32[]{:S(2)}) %collective-permute-start.6) | collective-permute-done | bytes 1056 | tf_op jit(solution)/shard_map/ppermute | solution.py:14
  53.3 1.3 collective-permute-start.7
  54.6 3.8 %collective-permute-done.7 = s32[256]{0:T(256)S(1)} collective-permute-done((s32[256]{0:T(256)S(1)}, s32[256]{0:T(256)S(1)}, u32[]{:S(2)}, u32[]{:S(2)}) %collective-permute-start.7) | collective-permute-done | bytes 1056 | tf_op jit(solution)/shard_map/ppermute | solution.py:14
  58.3 1.0 fusion.12
  59.3 1.0 constant_dynamic-update-slice_fusion.3
  60.5 1.0 fusion.54
  61.5 2.9 %exponential_reduce_fusion = f32[4,256]{1,0:T(4,128)S(1)} fusion(pred[256,1280]{1,0:T(8,128)(4,1)S(1)} %copy-done.3, bf16[256,4,80]{0,2,1:T(8,128)(2,1)} %bitcast.38, bf16[1280,4,80]{0,2,1:T(8,128)(2,1)S(1)} %bitcast.31), kind=kOutput, calls=%fused_computation.6 | convolution fusion | flops 214959360 | bytes 1314816 | tf_op jit(solution)/shard_map/sub | solution.py:74
  64.4 4.1 %fusion.13 = bf16[4,80,256]{2,1,0:T(8,128)(2,1)} fusion(bf16[1280,4,80]{0,2,1:T(8,128)(2,1)} %bitcast.33, f32[4,256]{1,0:T(4,128)S(1)} %exponential_reduce_fusion, pred[256,1280]{1,0:T(8,128)(4,1)S(1)} %copy-done.3, bf16[256,4,80]{0,2,1:T(8,128)(2,1)} %bitcast.39, bf16[1280,4,80]{0,2,1:T(8,128)(2,1)S(1)} %bitcast.32), kind=kOutput, calls=%fused_computation.22 | convolution fusion | flops 426068224 | bytes 2297856 | tf_op jit(solution)/shard_map/hqk,khd->qhd/dot_general | solution.py:77
  68.6 1.2 copy.33
  69.7 1.2 gather_fusion.1
  70.9 1.4 convolution_convert_fusion
  72.7 0.7 gather_fusion
  73.6 34.7 %reduce-scatter.5.cloned.1.call-done = bf16[64,1280]{1,0:T(8,128)(2,1)} async-done(((bf16[256,1280]{1,0:T(8,128)(2,1)}), bf16[64,1280]{1,0:T(8,128)(2,1)}) %reduce-scatter.5.cloned.1.call-update) | async-done | bytes 163856 | tf_op jit(solution)/shard_map/reduce_scatter | solution.py:85
  108.3 1.1 fusion.18
  109.5 1.2 multiply_reduce_fusion
  110.7 1.4 convolution_convert_fusion.5
  112.1 0.8 copy.36
  113.3 25.1 %reduce-scatter.7.cloned.1.call-done = bf16[160,64]{1,0:T(8,128)(2,1)} async-done(((bf16[640,64]{1,0:T(8,128)(2,1)}), bf16[160,64]{1,0:T(8,128)(2,1)}) %reduce-scatter.7.cloned.1.call-update) | async-done | bytes 20496
  138.4 1.0 convolution_convert_fusion.4
  140.0 28.9 %all_to_all.6 = bf16[128,2,240]{2,1,0:T(2,128)(2,1)S(1)} all-to-all(bf16[128,2,240]{2,1,0:T(2,128)(2,1)S(1)} %reshape.225), channel_id=1, replica_groups=mesh['seq'=128,'tp'=4] {'seq'}, dimensions={0} | all-to-all | bytes 245760 | tf_op jit(solution)/shard_map/all_to_all | solution.py:114
  169.7 0.8 convolution_convert_fusion.6
  (75 shorter events, 4.5 us)
Async XLA Ops:
  6.5 104.2 %copy-start = (bf16[1280,640]{1,0:T(8,128)(2,1)S(1)}, bf16[1280,640]{1,0:T(8,128)(2,1)}, u32[]{:S(2)}) copy-start(bf16[1280,640]{1,0:T(8,128)(2,1)} %param.23) | copy-start | bytes 4915204
  6.5 12.1 %copy-start.10 = (f32[1280]{0:T(1024)S(1)}, f32[1280]{0:T(1024)}, u32[]{:S(2)}) copy-start(f32[1280]{0:T(1024)} %param.15) | copy-start | bytes 15364
  6.5 12.1 %copy-start.8 = (bf16[1280,320]{0,1:T(8,128)(2,1)S(1)}, bf16[1280,320]{0,1:T(8,128)(2,1)}, u32[]{:S(2)}) copy-start(bf16[1280,320]{0,1:T(8,128)(2,1)} %param.17) | copy-start | bytes 2457604
  6.5 101.8 %reduce-scatter.5.cloned.1.call-start = ((), (), s32[]{:S(2)}) async-start(), calls=%async_computation.3 | async-start | bytes 819200 | tf_op jit(solution)/shard_map/reduce_scatter | solution.py:85
  18.4 1.1 copy-start.9
  19.6 16.5 %copy-start.6 = (s32[256]{0:T(256)S(1)}, s32[256]{0:T(256)}, u32[]{:S(2)}) copy-start(s32[256]{0:T(256)} %param.20) | copy-start | bytes 3076
  19.6 16.5 %copy-start.7 = (s32[256]{0:T(256)S(1)}, s32[256]{0:T(256)}, u32[]{:S(2)}) copy-start(s32[256]{0:T(256)} %param.21) | copy-start | bytes 3076
  19.6 20.4 %copy-start.5 = (s32[64,4]{0,1:T(4,128)S(1)}, s32[64,4]{0,1:T(4,128)}, u32[]{:S(2)}) copy-start(s32[64,4]{0,1:T(4,128)} %param.24) | copy-start | bytes 3076
  20.9 38.4 %collective-permute-start = (bf16[256,640]{0,1:T(8,128)(2,1)}, bf16[256,640]{0,1:T(8,128)(2,1)}, u32[]{:S(2)}, u32[]{:S(2)}) collective-permute-start(bf16[256,640]{0,1:T(8,128)(2,1)} %get-tuple-element.23), channel_id=1, source_target_pairs={{0,4},{4,8},{8,12},{12,16},{16,20},{20,24},{24,28},{28,32},{32,36}... | collective-permute-start | bytes 983048 | tf_op jit(solution)/shard_map/ppermute | solution.py:14
  28.4 31.9 %collective-permute-start.1 = (bf16[256,640]{0,1:T(8,128)(2,1)}, bf16[256,640]{0,1:T(8,128)(2,1)S(1)}, u32[]{:S(2)}, u32[]{:S(2)}) collective-permute-start(bf16[256,640]{0,1:T(8,128)(2,1)} %get-tuple-element.23), channel_id=1, source_target_pairs={{0,8},{4,12},{8,16},{12,20},{16,24},{20,28},{24,32},{28,36},{32,40... | collective-permute-start | bytes 983048 | tf_op jit(solution)/shard_map/ppermute | solution.py:14
  32.4 28.0 %collective-permute-start.2 = (bf16[256,640]{0,1:T(8,128)(2,1)}, bf16[256,640]{0,1:T(8,128)(2,1)S(1)}, u32[]{:S(2)}, u32[]{:S(2)}) collective-permute-start(bf16[256,640]{0,1:T(8,128)(2,1)} %get-tuple-element.23), channel_id=1, source_target_pairs={{4,0},{8,4},{12,8},{16,12},{20,16},{24,20},{28,24},{32,28},{36,32}... | collective-permute-start | bytes 983048 | tf_op jit(solution)/shard_map/ppermute | solution.py:14
  34.7 25.7 %collective-permute-start.3 = (bf16[256,640]{0,1:T(8,128)(2,1)}, bf16[256,640]{0,1:T(8,128)(2,1)S(1)}, u32[]{:S(2)}, u32[]{:S(2)}) collective-permute-start(bf16[256,640]{0,1:T(8,128)(2,1)} %get-tuple-element.23), channel_id=1, source_target_pairs={{8,0},{12,4},{16,8},{20,12},{24,16},{28,20},{32,24},{36,28},{40,32... | collective-permute-start | bytes 983048 | tf_op jit(solution)/shard_map/ppermute | solution.py:14
  36.1 6.5 %collective-permute-start.4 = (s32[256]{0:T(256)S(1)}, s32[256]{0:T(256)S(1)}, u32[]{:S(2)}, u32[]{:S(2)}) collective-permute-start(s32[256]{0:T(256)S(1)} %get-tuple-element.20), channel_id=1, source_target_pairs={{0,4},{4,8},{8,12},{12,16},{16,20},{20,24},{24,28},{28,32},{32,36}... | collective-permute-start | bytes 3080 | tf_op jit(solution)/shard_map/ppermute | solution.py:14
  40.2 19.2 %copy-start.1 = (bf16[1280,640]{0,1:T(8,128)(2,1)S(1)}, bf16[1280,640]{0,1:T(8,128)(2,1)}, u32[]{:S(2)}) copy-start(bf16[1280,640]{0,1:T(8,128)(2,1)} %get-tuple-element.24) | copy-start | bytes 4915204
  42.6 4.7 %collective-permute-start.5 = (s32[256]{0:T(256)S(1)}, s32[256]{0:T(256)S(1)}, u32[]{:S(2)}, u32[]{:S(2)}) collective-permute-start(s32[256]{0:T(256)S(1)} %get-tuple-element.20), channel_id=1, source_target_pairs={{0,8},{4,12},{8,16},{12,20},{16,24},{20,28},{24,32},{28,36},{32,40... | collective-permute-start | bytes 3080 | tf_op jit(solution)/shard_map/ppermute | solution.py:14
  47.3 6.0 %collective-permute-start.6 = (s32[256]{0:T(256)S(1)}, s32[256]{0:T(256)S(1)}, u32[]{:S(2)}, u32[]{:S(2)}) collective-permute-start(s32[256]{0:T(256)S(1)} %get-tuple-element.20), channel_id=1, source_target_pairs={{4,0},{8,4},{12,8},{16,12},{20,16},{24,20},{28,24},{32,28},{36,32}... | collective-permute-start | bytes 3080 | tf_op jit(solution)/shard_map/ppermute | solution.py:14
  53.3 5.1 %collective-permute-start.7 = (s32[256]{0:T(256)S(1)}, s32[256]{0:T(256)S(1)}, u32[]{:S(2)}, u32[]{:S(2)}) collective-permute-start(s32[256]{0:T(256)S(1)} %get-tuple-element.20), channel_id=1, source_target_pairs={{8,0},{12,4},{16,8},{20,12},{24,16},{28,20},{32,24},{36,28},{40,32... | collective-permute-start | bytes 3080 | tf_op jit(solution)/shard_map/ppermute | solution.py:14
  60.5 1.0 copy-start.3
  68.6 2.3 %copy-start.2 = (bf16[320,1280]{1,0:T(8,128)(2,1)S(1)}, bf16[320,1280]{1,0:T(8,128)(2,1)}, u32[]{:S(2)}) copy-start(bf16[320,1280]{1,0:T(8,128)(2,1)} %param.19) | copy-start | bytes 2457604
  72.3 1.1 copy-start.11
  72.3 38.4 %copy-start.4 = (f32[1280]{0:T(1024)S(1)}, f32[1280]{0:T(1024)}, u32[]{:S(2)}) copy-start(f32[1280]{0:T(1024)} %param.22) | copy-start | bytes 15364
  72.3 66.1 %reduce-scatter.7.cloned.1.call-start = ((), (), s32[]{:S(2)}) async-start(), calls=%async_computation.4 | async-start | bytes 204800
Sparse Core Ops, SparseCore 0:
  72.4 35.8 reduce-scatter.4
  113.0 25.2 reduce-scatter.6
where the time goes:
time: 178 us; the launch traced here: 177 us
  waiting for transfers between devices  68.4 us (38%)
  blocking collectives  40.5 us (23%)
  starting transfers between devices  26.1 us (15%)
  matrix products  15.1 us (8%)
  between operations  13.8 us (8%)
  local copies, waits for them, and re-layouts  7.86 us (4%)
  other arithmetic  5.42 us (3%)
    reduce_scatter x1, waiting for transfers between devices, body(): lax.psum_scatter(partial_sum.astype(jnp.bfloat16), 'tp', scatter_dimensio...  34.7 us
    all_to_all x1, blocking collectives, body(): lax.all_to_all(send_buf, 'seq', 0, 0, tiled=True)  28.9 us
    ppermute x8, starting transfers between devices, from_behind(): return lax.ppermute(shard, axis, pairs)  26.1 us
    unnamed x3, waiting for transfers between devices  25.1 us
    all_gather x1, blocking collectives, body(): gathered = lax.all_gather(tokens, 'tp', axis=1, tiled=True)  11.7 us
    ppermute x8, waiting for transfers between devices, from_behind(): return lax.ppermute(shard, axis, pairs)  8.52 us
    dot_general x1, matrix products, body(): jnp.einsum('hqk,khd->qhd', weights, value_heads, preferred_element_type=j...  4.14 us
  transfers between devices with their start and end apart: 10, of which 5 were waited for; matrix products, arithmetic and copies ran while one was open for 4% of the time, Pallas kernels for 0%

commit v1 on v0

--- a/solution.py
+++ b/solution.py
@@ -6,6 +6,12 @@
 HD = 80
 CAP = 2
 EPS = 1e-06
+
+
+def core_cut(z_in, chip_axis):
+    return jnp.concatenate(
+        lax.all_to_all(jnp.stack([z_in] * lax.axis_size(chip_axis), 0), chip_axis, 0, 0), axis=1
+    )
 
 
 def from_behind(shard, axis, by):
@@ -41,7 +47,7 @@
     heads_here = local_width // HD
     tp_size = lax.axis_size("tp")
     seq_size = lax.axis_size("seq")
-    gathered = lax.all_gather(tokens, "tp", axis=1, tiled=True)
+    gathered = core_cut(tokens, "tp")
     normed = layer_norm(gathered, first_gain).astype(jnp.bfloat16)
     queries = jnp.dot(normed, w_query, preferred_element_type=jnp.float32).astype(jnp.bfloat16)
     key_rows = jnp.dot(normed, w_key, preferred_element_type=jnp.float32).astype(jnp.bfloat16)

time: 178 us -> 172 us (0.966)
  blocking collectives: 40.5 us -> 28.9 us
  starting transfers between devices: 26.1 us -> 29.7 us
  waiting for transfers between devices: 68.4 us -> 71.5 us
    all_gather x1 -> x0, blocking collectives: 11.7 us -> none  [body(): gathered = lax.all_gather(tokens, 'tp', axis=1, tiled=True)]
    all_to_all x0 -> x1, waiting for transfers between devices: none -> 10.2 us  [core_cut(): lax.all_to_all(jnp.stack([z_in] * lax.axis_size(chip_axis), 0), chip_axis...]
    reduce_scatter x1, waiting for transfers between devices: 34.7 us -> 25.6 us  [body(): lax.psum_scatter(partial_sum.astype(jnp.bfloat16), 'tp', scatter_dimensio...]
    all_to_all x0 -> x1, starting transfers between devices: none -> 3.98 us  [core_cut(): lax.all_to_all(jnp.stack([z_in] * lax.axis_size(chip_axis), 0), chip_axis...]
    ppermute x8, waiting for transfers between devices: 8.52 us -> 10.6 us  [from_behind(): return lax.ppermute(shard, axis, pairs)]
    another operation x0 -> x1, local copies, waits for them, and re-layouts: none -> 1.79 us  [core_cut(): jnp.stack([z_in] * lax.axis_size(chip_axis), 0)]
  transfers between devices with their start and end apart: 10 -> 11, of which waited for: 5 -> 6; matrix products, arithmetic and copies ran while one was open for 4% -> 3% of each run, Pallas kernels for 0% -> 0%
where the time goes in v1:
time: 172 us; the launch traced here: 171 us
  waiting for transfers between devices  71.5 us (42%)
  starting transfers between devices  29.7 us (17%)
  blocking collectives  28.9 us (17%)
  between operations  13.8 us (8%)
  matrix products  13.5 us (8%)
  local copies, waits for them, and re-layouts  8.77 us (5%)
  other arithmetic  4.9 us (3%)
    all_to_all x1, blocking collectives, body(): lax.all_to_all(send_buf, 'seq', 0, 0, tiled=True)  28.9 us
    ppermute x8, starting transfers between devices, from_behind(): return lax.ppermute(shard, axis, pairs)  25.6 us
    reduce_scatter x1, waiting for transfers between devices, body(): lax.psum_scatter(partial_sum.astype(jnp.bfloat16), 'tp', scatter_dimensio...  25.6 us
    unnamed x3, waiting for transfers between devices  25.1 us
    ppermute x8, waiting for transfers between devices, from_behind(): return lax.ppermute(shard, axis, pairs)  10.6 us
    all_to_all x1, waiting for transfers between devices, core_cut(): lax.all_to_all(jnp.stack([z_in] * lax.axis_size(chip_axis), 0), chip_axis...  10.2 us
    dot_general x1, matrix products, body(): jnp.einsum('hqk,khd->qhd', weights, value_heads, preferred_element_type=j...  4.14 us
    all_to_all x1, starting transfers between devices, core_cut(): lax.all_to_all(jnp.stack([z_in] * lax.axis_size(chip_axis), 0), chip_axis...  3.98 us
  transfers between devices with their start and end apart: 11, of which 6 were waited for; matrix products, arithmetic and copies ran while one was open for 3% of the time, Pallas kernels for 0%

profile of v1, /device:TPU:1, one launch (start us, length us, event | category | flops | bytes accessed | tf_op | source)
XLA Modules:
  0.0 171.0 jit_solution(2077703551842062875)
XLA Ops:
  6.5 0.8 constant_dynamic-update-slice_fusion.5
  7.4 5.5 %collective-permute-start.4 = (s32[256]{0:T(256)S(1)}, s32[256]{0:T(256)S(1)}, u32[]{:S(2)}, u32[]{:S(2)}) collective-permute-start(s32[256]{0:T(256)S(1)} %get-tuple-element.20), channel_id=1, source_target_pairs={{0,4},{4,8},{8,12},{12,16},{16,20},{20,24},{24,28},{28,32},{32,36}... | collective-permute-start | bytes 3080 | tf_op jit(solution)/shard_map/ppermute | solution.py:20
  12.9 4.0 %collective-permute-start.5 = (s32[256]{0:T(256)S(1)}, s32[256]{0:T(256)S(1)}, u32[]{:S(2)}, u32[]{:S(2)}) collective-permute-start(s32[256]{0:T(256)S(1)} %get-tuple-element.20), channel_id=1, source_target_pairs={{0,8},{4,12},{8,16},{12,20},{16,24},{20,28},{24,32},{28,36},{32,40... | collective-permute-start | bytes 3080 | tf_op jit(solution)/shard_map/ppermute | solution.py:20
  16.9 2.0 %collective-permute-start.6 = (s32[256]{0:T(256)S(1)}, s32[256]{0:T(256)S(1)}, u32[]{:S(2)}, u32[]{:S(2)}) collective-permute-start(s32[256]{0:T(256)S(1)} %get-tuple-element.20), channel_id=1, source_target_pairs={{4,0},{8,4},{12,8},{16,12},{20,16},{24,20},{28,24},{32,28},{36,32}... | collective-permute-start | bytes 3080 | tf_op jit(solution)/shard_map/ppermute | solution.py:20
  18.8 1.3 collective-permute-start.7
  20.1 1.8 %stack.2 = bf16[4,256,320]{1,2,0:T(8,128)(2,1)} broadcast(bf16[256,320]{0,1:T(8,128)(2,1)} %param.14), dimensions={1,2} | broadcast | bytes 819200 | tf_op jit(solution)/shard_map/stack | solution.py:13
  21.9 4.0 %all-to-all-start = ((bf16[4,256,320]{1,2,0:T(8,128)(2,1)}), bf16[4,256,320]{1,2,0:T(8,128)(2,1)S(1)}, u32[]{:S(2)}, u32[]{:S(2)}) async-start(bf16[4,256,320]{1,2,0:T(8,128)(2,1)} %stack.2), calls=%async_computation | async-start | bytes 1310720 | tf_op jit(solution)/shard_map/all_to_all | solution.py:13
  26.2 10.2 %all-to-all-done = bf16[4,256,320]{1,2,0:T(8,128)(2,1)S(1)} async-done(((bf16[4,256,320]{1,2,0:T(8,128)(2,1)}), bf16[4,256,320]{1,2,0:T(8,128)(2,1)S(1)}, u32[]{:S(2)}, u32[]{:S(2)}) %all-to-all-start) | async-done | bytes 655392 | tf_op jit(solution)/shard_map/all_to_all | solution.py:13
  38.4 5.9 %collective-permute-start = (bf16[256,640]{0,1:T(8,128)(2,1)S(1)}, bf16[256,640]{0,1:T(8,128)(2,1)S(1)}, u32[]{:S(2)}, u32[]{:S(2)}) collective-permute-start(bf16[256,640]{0,1:T(8,128)(2,1)S(1)} %get-tuple-element.23), channel_id=1, source_target_pairs={{0,4},{4,8},{8,12},{12,16},{16,20},{20,24},{24,28},{28,32},{32,36}... | collective-permute-start | bytes 983048 | tf_op jit(solution)/shard_map/ppermute | solution.py:20
  44.6 3.8 %collective-permute-start.1 = (bf16[256,640]{0,1:T(8,128)(2,1)S(1)}, bf16[256,640]{0,1:T(8,128)(2,1)S(1)}, u32[]{:S(2)}, u32[]{:S(2)}) collective-permute-start(bf16[256,640]{0,1:T(8,128)(2,1)S(1)} %get-tuple-element.23), channel_id=1, source_target_pairs={{0,8},{4,12},{8,16},{12,20},{16,24},{20,28},{24,32},{28,36},{32,40... | collective-permute-start | bytes 983048 | tf_op jit(solution)/shard_map/ppermute | solution.py:20
  48.4 1.9 %collective-permute-start.2 = (bf16[256,640]{0,1:T(8,128)(2,1)S(1)}, bf16[256,640]{0,1:T(8,128)(2,1)S(1)}, u32[]{:S(2)}, u32[]{:S(2)}) collective-permute-start(bf16[256,640]{0,1:T(8,128)(2,1)S(1)} %get-tuple-element.23), channel_id=1, source_target_pairs={{4,0},{8,4},{12,8},{16,12},{20,16},{24,20},{28,24},{32,28},{36,32}... | collective-permute-start | bytes 983048 | tf_op jit(solution)/shard_map/ppermute | solution.py:20
  50.3 1.3 collective-permute-start.3
  51.6 1.1 convolution_convert_fusion.1
  52.7 2.6 %collective-permute-done.1 = bf16[256,640]{0,1:T(8,128)(2,1)S(1)} collective-permute-done((bf16[256,640]{0,1:T(8,128)(2,1)S(1)}, bf16[256,640]{0,1:T(8,128)(2,1)S(1)}, u32[]{:S(2)}, u32[]{:S(2)}) %collective-permute-start.1) | collective-permute-done | bytes 327712 | tf_op jit(solution)/shard_map/ppermute | solution.py:20
  55.3 2.1 %collective-permute-done.2 = bf16[256,640]{0,1:T(8,128)(2,1)S(1)} collective-permute-done((bf16[256,640]{0,1:T(8,128)(2,1)S(1)}, bf16[256,640]{0,1:T(8,128)(2,1)S(1)}, u32[]{:S(2)}, u32[]{:S(2)}) %collective-permute-start.2) | collective-permute-done | bytes 327712 | tf_op jit(solution)/shard_map/ppermute | solution.py:20
  57.5 5.8 %collective-permute-done.3 = bf16[256,640]{0,1:T(8,128)(2,1)S(1)} collective-permute-done((bf16[256,640]{0,1:T(8,128)(2,1)S(1)}, bf16[256,640]{0,1:T(8,128)(2,1)S(1)}, u32[]{:S(2)}, u32[]{:S(2)}) %collective-permute-start.3) | collective-permute-done | bytes 327712 | tf_op jit(solution)/shard_map/ppermute | solution.py:20
  63.4 1.0 fusion.48
  64.4 2.9 %exponential_reduce_fusion = f32[4,256]{1,0:T(4,128)S(1)} fusion(pred[256,1280]{1,0:T(8,128)(4,1)S(1)} %fusion.9, bf16[256,4,80]{0,2,1:T(8,128)(2,1)} %bitcast.45, bf16[1280,4,80]{0,2,1:T(8,128)(2,1)S(1)} %bitcast.41), kind=kOutput, calls=%fused_computation.6 | convolution fusion | flops 214959360 | bytes 1314816 | tf_op jit(solution)/shard_map/sub | solution.py:80
  67.3 4.1 %fusion.10 = bf16[4,80,256]{2,1,0:T(8,128)(2,1)} fusion(bf16[1280,4,80]{0,2,1:T(8,128)(2,1)} %bitcast.43, f32[4,256]{1,0:T(4,128)S(1)} %exponential_reduce_fusion, pred[256,1280]{1,0:T(8,128)(4,1)S(1)} %fusion.9, bf16[256,4,80]{0,2,1:T(8,128)(2,1)} %bitcast.46, bf16[1280,4,80]{0,2,1:T(8,128)(2,1)S(1)} %bitcast.42), kind=kOutput, calls=%fused_computation.20 | convolution fusion | flops 426068224 | bytes 2297856 | tf_op jit(solution)/shard_map/hqk,khd->qhd/dot_general | solution.py:83
  71.4 1.2 copy.33
  72.6 1.2 gather_fusion.1
  73.8 1.4 convolution_convert_fusion
  75.8 0.7 gather_fusion
  76.5 25.6 %reduce-scatter.5.cloned.1.call-done = bf16[64,1280]{1,0:T(8,128)(2,1)} async-done(((bf16[256,1280]{1,0:T(8,128)(2,1)}), bf16[64,1280]{1,0:T(8,128)(2,1)}) %reduce-scatter.5.cloned.1.call-update) | async-done | bytes 163856 | tf_op jit(solution)/shard_map/reduce_scatter | solution.py:91
  102.1 1.1 fusion.15
  103.3 1.2 multiply_reduce_fusion
  104.5 1.4 convolution_convert_fusion.5
  105.9 0.8 copy.36
  107.1 25.0 %reduce-scatter.7.cloned.1.call-done = bf16[160,64]{1,0:T(8,128)(2,1)} async-done(((bf16[640,64]{1,0:T(8,128)(2,1)}), bf16[160,64]{1,0:T(8,128)(2,1)}) %reduce-scatter.7.cloned.1.call-update) | async-done | bytes 20496
  132.1 0.9 convolution_convert_fusion.4
  133.7 28.9 %all_to_all.11 = bf16[128,2,240]{2,1,0:T(2,128)(2,1)S(1)} all-to-all(bf16[128,2,240]{2,1,0:T(2,128)(2,1)S(1)} %reshape.240), channel_id=1, replica_groups=mesh['seq'=128,'tp'=4] {'seq'}, dimensions={0} | all-to-all | bytes 245760 | tf_op jit(solution)/shard_map/all_to_all | solution.py:120
  163.4 0.8 convolution_convert_fusion.6
  (72 shorter events, 4.9 us)
Async XLA Ops:
  6.5 98.0 %copy-start = (bf16[1280,640]{1,0:T(8,128)(2,1)S(1)}, bf16[1280,640]{1,0:T(8,128)(2,1)}, u32[]{:S(2)}) copy-start(bf16[1280,640]{1,0:T(8,128)(2,1)} %param.23) | copy-start | bytes 4915204
  6.5 19.4 %copy-start.7 = (s32[64,4]{0,1:T(4,128)S(1)}, s32[64,4]{0,1:T(4,128)}, u32[]{:S(2)}) copy-start(s32[64,4]{0,1:T(4,128)} %param.24) | copy-start | bytes 3076
  7.4 29.5 %copy-start.5 = (f32[1280]{0:T(1024)S(1)}, f32[1280]{0:T(1024)}, u32[]{:S(2)}) copy-start(f32[1280]{0:T(1024)} %param.15) | copy-start | bytes 15364
  7.4 18.8 %collective-permute-start.4 = (s32[256]{0:T(256)S(1)}, s32[256]{0:T(256)S(1)}, u32[]{:S(2)}, u32[]{:S(2)}) collective-permute-start(s32[256]{0:T(256)S(1)} %get-tuple-element.20), channel_id=1, source_target_pairs={{0,4},{4,8},{8,12},{12,16},{16,20},{20,24},{24,28},{28,32},{32,36}... | collective-permute-start | bytes 3080 | tf_op jit(solution)/shard_map/ppermute | solution.py:20
  12.9 13.3 %collective-permute-start.5 = (s32[256]{0:T(256)S(1)}, s32[256]{0:T(256)S(1)}, u32[]{:S(2)}, u32[]{:S(2)}) collective-permute-start(s32[256]{0:T(256)S(1)} %get-tuple-element.20), channel_id=1, source_target_pairs={{0,8},{4,12},{8,16},{12,20},{16,24},{20,28},{24,32},{28,36},{32,40... | collective-permute-start | bytes 3080 | tf_op jit(solution)/shard_map/ppermute | solution.py:20
  16.9 9.3 %collective-permute-start.6 = (s32[256]{0:T(256)S(1)}, s32[256]{0:T(256)S(1)}, u32[]{:S(2)}, u32[]{:S(2)}) collective-permute-start(s32[256]{0:T(256)S(1)} %get-tuple-element.20), channel_id=1, source_target_pairs={{4,0},{8,4},{12,8},{16,12},{20,16},{24,20},{28,24},{32,28},{36,32}... | collective-permute-start | bytes 3080 | tf_op jit(solution)/shard_map/ppermute | solution.py:20
  18.8 7.4 %collective-permute-start.7 = (s32[256]{0:T(256)S(1)}, s32[256]{0:T(256)S(1)}, u32[]{:S(2)}, u32[]{:S(2)}) collective-permute-start(s32[256]{0:T(256)S(1)} %get-tuple-element.20), channel_id=1, source_target_pairs={{8,0},{12,4},{16,8},{20,12},{24,16},{28,20},{32,24},{36,28},{40,32... | collective-permute-start | bytes 3080 | tf_op jit(solution)/shard_map/ppermute | solution.py:20
  21.9 14.4 %all-to-all-start = ((bf16[4,256,320]{1,2,0:T(8,128)(2,1)}), bf16[4,256,320]{1,2,0:T(8,128)(2,1)S(1)}, u32[]{:S(2)}, u32[]{:S(2)}) async-start(bf16[4,256,320]{1,2,0:T(8,128)(2,1)} %stack.2), calls=%async_computation | async-start | bytes 1310720 | tf_op jit(solution)/shard_map/all_to_all | solution.py:13
  25.9 11.2 %copy-start.1 = (bf16[1280,320]{0,1:T(8,128)(2,1)S(1)}, bf16[1280,320]{0,1:T(8,128)(2,1)}, u32[]{:S(2)}) copy-start(bf16[1280,320]{0,1:T(8,128)(2,1)} %param.18) | copy-start | bytes 2457604
  25.9 76.2 %reduce-scatter.5.cloned.1.call-start = ((), (), s32[]{:S(2)}) async-start(), calls=%async_computation.4 | async-start | bytes 819200 | tf_op jit(solution)/shard_map/reduce_scatter | solution.py:91
  36.8 1.1 copy-start.2
  38.0 13.6 %copy-start.3 = (bf16[1280,320]{0,1:T(8,128)(2,1)S(1)}, bf16[1280,320]{0,1:T(8,128)(2,1)}, u32[]{:S(2)}) copy-start(bf16[1280,320]{0,1:T(8,128)(2,1)} %param.16) | copy-start | bytes 2457604
  38.4 14.3 %collective-permute-start = (bf16[256,640]{0,1:T(8,128)(2,1)S(1)}, bf16[256,640]{0,1:T(8,128)(2,1)S(1)}, u32[]{:S(2)}, u32[]{:S(2)}) collective-permute-start(bf16[256,640]{0,1:T(8,128)(2,1)S(1)} %get-tuple-element.23), channel_id=1, source_target_pairs={{0,4},{4,8},{8,12},{12,16},{16,20},{20,24},{24,28},{28,32},{32,36}... | collective-permute-start | bytes 983048 | tf_op jit(solution)/shard_map/ppermute | solution.py:20
  44.6 10.8 %collective-permute-start.1 = (bf16[256,640]{0,1:T(8,128)(2,1)S(1)}, bf16[256,640]{0,1:T(8,128)(2,1)S(1)}, u32[]{:S(2)}, u32[]{:S(2)}) collective-permute-start(bf16[256,640]{0,1:T(8,128)(2,1)S(1)} %get-tuple-element.23), channel_id=1, source_target_pairs={{0,8},{4,12},{8,16},{12,20},{16,24},{20,28},{24,32},{28,36},{32,40... | collective-permute-start | bytes 983048 | tf_op jit(solution)/shard_map/ppermute | solution.py:20
  48.4 9.1 %collective-permute-start.2 = (bf16[256,640]{0,1:T(8,128)(2,1)S(1)}, bf16[256,640]{0,1:T(8,128)(2,1)S(1)}, u32[]{:S(2)}, u32[]{:S(2)}) collective-permute-start(bf16[256,640]{0,1:T(8,128)(2,1)S(1)} %get-tuple-element.23), channel_id=1, source_target_pairs={{4,0},{8,4},{12,8},{16,12},{20,16},{24,20},{28,24},{32,28},{36,32}... | collective-permute-start | bytes 983048 | tf_op jit(solution)/shard_map/ppermute | solution.py:20
  50.3 13.0 %collective-permute-start.3 = (bf16[256,640]{0,1:T(8,128)(2,1)S(1)}, bf16[256,640]{0,1:T(8,128)(2,1)S(1)}, u32[]{:S(2)}, u32[]{:S(2)}) collective-permute-start(bf16[256,640]{0,1:T(8,128)(2,1)S(1)} %get-tuple-element.23), channel_id=1, source_target_pairs={{8,0},{12,4},{16,8},{20,12},{24,16},{28,20},{32,24},{36,28},{40,32... | collective-permute-start | bytes 983048 | tf_op jit(solution)/shard_map/ppermute | solution.py:20
  71.4 2.3 %copy-start.4 = (bf16[320,1280]{1,0:T(8,128)(2,1)S(1)}, bf16[320,1280]{1,0:T(8,128)(2,1)}, u32[]{:S(2)}) copy-start(bf16[320,1280]{1,0:T(8,128)(2,1)} %param.19) | copy-start | bytes 2457604
  72.6 2.7 %copy-start.8 = (s32[64]{0:T(128)S(1)}, s32[64]{0:T(128)}, u32[]{:S(2)}) copy-start(s32[64]{0:T(128)} %param.25) | copy-start | bytes 772
  75.2 56.9 %reduce-scatter.7.cloned.1.call-start = ((), (), s32[]{:S(2)}) async-start(), calls=%async_computation.5 | async-start | bytes 204800
  75.5 29.0 %copy-start.6 = (f32[1280]{0:T(1024)S(1)}, f32[1280]{0:T(1024)}, u32[]{:S(2)}) copy-start(f32[1280]{0:T(1024)} %param.22) | copy-start | bytes 15364
Sparse Core Ops, SparseCore 0:
  75.3 26.7 reduce-scatter.4
  106.8 25.2 reduce-scatter.6
